TPU v7x, 512 devices: a whole 4x8x8 slice. The times are simulated.
512 devices in a mesh: rep: 8 (over y_lo, core), seq: 2 (over y_hi), tp: 32 (over x, z).
Axes of the slice: x: 4, y: 8 (y_hi: 2, y_lo: 4; y = y_hi * 4 + y_lo), z: 8, core: 2. Of those that a mesh axis runs over, the one named last changes fastest.
Arguments:
- hidden: bfloat16 [3072, 8192], P('rep', ('seq', 'tp')), may hold values from -100 to 100
- gain: float32 [8192], replicated, may hold values from 0.1 to 1.9
- w_query: bfloat16 [8192, 8192], P('seq', 'tp'), may hold values from -1 to 1
- w_keyval: bfloat16 [2, 4096, 2048], P(None, 'tp'), may hold values from -1 to 1
- lengths: int32 [8, 2], replicated, may hold values from 128 to 192, as said below
- routes: int32 [8, 2], replicated, may hold values from 0 to 7, as said below
Outputs:
- attended: bfloat16 [3072, 8192], P(('rep', 'seq'), 'tp')
Inputs may be any that keep to these rules, and one draw needn't show every extreme that they name: `routes`: for each j, the responses j of the 8 rollout groups go to 8 different replicas, so each replica receives exactly 2 responses. `lengths`: the responses that one rollout group sends to one replica hold at most 192 tokens together, and in every draw some group sends exactly 192 tokens to one replica.
All inputs are finite; a program needn't handle non-finite values.
Results may differ from a plain program's by a relative error of at most 0.0076.
Values may be sent and summed in bfloat16 or wider, within the bound.
No kernel may reach another device: no remote copies, remote signals or barrier semaphores. Data moves between devices by JAX's collectives and lax.ppermute only.
A program may use at most 64 MiB of HBM per device.

v0:
```python
import math
import jax
import jax.numpy as jnp
from jax import lax
from jax.sharding import PartitionSpec as P

D = 8192
QH = 64
KVH = 8
HD = 128
RESP = 2
LMAX = 192
BUFFER = 384
ROPE_BASE = 500000.0
NORM_EPS = 1e-05
MASK_FILL = -1e30


def response_tables(lengths, routes):
    flat_len = lengths.reshape(-1)
    flat_route = routes.reshape(-1)
    response_ids = jnp.arange(flat_len.shape[0], dtype=jnp.int32)
    group_of = response_ids // RESP
    same_route = flat_route[:, None] == flat_route[None, :]
    same_group = group_of[:, None] == group_of[None, :]
    earlier = response_ids[None, :] < response_ids[:, None]
    dest_off = jnp.sum(jnp.where(same_route & earlier, flat_len[None, :], 0), axis=1)
    pair_off = jnp.sum(jnp.where(same_route & same_group & earlier, flat_len[None, :], 0), axis=1)
    src_start = jnp.sum(jnp.where(same_group & earlier, flat_len[None, :], 0), axis=1)
    return (flat_len, flat_route, group_of, dest_off, pair_off, src_start)


def locate(positions, replica, tables):
    flat_len, flat_route, group_of, dest_off, pair_off, src_start = tables
    response_ids = jnp.arange(flat_len.shape[0], dtype=jnp.int32)
    position_col = positions[:, None]
    inside = (
        (flat_route[None, :] == replica)
        & (dest_off[None, :] <= position_col)
        & (position_col < dest_off[None, :] + flat_len[None, :])
    )
    inside_int = inside.astype(jnp.int32)
    segment = jnp.sum(inside_int * (response_ids[None, :] + 1), axis=1) - 1
    seg_start = jnp.sum(inside_int * dest_off[None, :], axis=1)
    source_group = jnp.sum(inside_int * group_of[None, :], axis=1)
    pair_first = jnp.sum(inside_int * (dest_off - pair_off)[None, :], axis=1)
    source = jnp.sum(inside_int * src_start[None, :], axis=1)
    within = jnp.where(segment >= 0, positions - seg_start, 0)
    return (segment, within, source_group, pair_first, source)


def rotary(values_in, within):
    head_dim = values_in.shape[-1]
    half_dim = head_dim // 2
    freq_index = jnp.arange(half_dim, dtype=jnp.float32)
    inverse = jnp.power(ROPE_BASE, -2.0 * freq_index / head_dim)
    angles = within.astype(jnp.float32)[:, None] * inverse[None, :]
    cosine = jnp.cos(angles)[:, None, :]
    sine_part = jnp.sin(angles)[:, None, :]
    lower_half = values_in[..., :half_dim]
    upper_half = values_in[..., half_dim:]
    return jnp.concatenate(
        [
            lower_half * cosine - upper_half * sine_part,
            upper_half * cosine + lower_half * sine_part,
        ],
        axis=-1,
    )


def fill_rows(table, indices, present):
    taken = jnp.take(table, indices.reshape(-1), axis=0)
    return jnp.where(present.reshape(-1)[:, None], taken, jnp.zeros((), table.dtype))


def local(hidden, gain, w_query, w_keyval, lengths, routes):
    rep_count = lax.axis_size("rep")
    seq_count = lax.axis_size("seq")
    replica = lax.axis_index("rep")
    seq_index = lax.axis_index("seq")
    column = lax.axis_index("tp")
    feature_cols = hidden.shape[1]
    local_rows = BUFFER // seq_count
    capacity = (RESP + rep_count - 1) // rep_count * LMAX
    head_count = w_query.shape[1] // HD
    tables = response_tables(lengths, routes)
    flat_len, flat_route, group_of, dest_off, pair_off, src_start = tables
    my_len = lax.dynamic_slice_in_dim(flat_len, replica * RESP, RESP)
    my_route = lax.dynamic_slice_in_dim(flat_route, replica * RESP, RESP)
    my_pair = lax.dynamic_slice_in_dim(pair_off, replica * RESP, RESP)
    my_start = lax.dynamic_slice_in_dim(src_start, replica * RESP, RESP)
    slot_ids = jnp.arange(capacity, dtype=jnp.int32)
    targets = jnp.arange(rep_count, dtype=jnp.int32)
    block_off = jnp.broadcast_to(slot_ids[None, :], (rep_count, capacity))
    offsets = block_off[:, :, None]
    inside = (
        (my_route[None, None, :] == targets[:, None, None])
        & (my_pair[None, None, :] <= offsets)
        & (offsets < (my_pair + my_len)[None, None, :])
    )
    inside_int = inside.astype(jnp.int32)
    src_rows = jnp.sum(
        inside_int * (my_start[None, None, :] + offsets - my_pair[None, None, :]), axis=2
    )
    src_rows, present = (src_rows, jnp.any(inside, axis=2))
    outgoing = fill_rows(hidden, src_rows, present)
    incoming = lax.all_to_all(outgoing, "rep", split_axis=0, concat_axis=0, tiled=True)
    all_pos = jnp.arange(BUFFER, dtype=jnp.int32)
    segment, within, source_group, pair_first, source = locate(all_pos, replica, tables)
    gathered_idx = jnp.where(segment >= 0, source_group * capacity + all_pos - pair_first, 0)
    assembled = fill_rows(incoming, gathered_idx, segment >= 0)
    local_x = lax.all_to_all(
        assembled.reshape(BUFFER, 1, feature_cols), "seq", split_axis=0, concat_axis=1, tiled=True
    )
    query_pos = seq_index * local_rows + jnp.arange(local_rows, dtype=jnp.int32)
    query_info = locate(query_pos, replica, tables)
    query_seg = query_info[0]
    query_within = query_info[1]
    query_valid = query_seg >= 0
    gain_halves = gain.reshape(seq_count, D // seq_count)
    gain_local = lax.dynamic_slice_in_dim(gain_halves, column * feature_cols, feature_cols, 1)
    kv_head = column * head_count // (QH // KVH)
    query_weights = lax.all_gather(
        w_query.reshape(1, w_query.shape[0], w_query.shape[1]), "seq", axis=0, tiled=True
    )
    feature_piece = lax.all_gather(local_x, "tp", axis=2, tiled=True)
    scaled_piece = (feature_piece.astype(jnp.float32) * gain_halves[None]).astype(jnp.bfloat16)
    query_acc = jnp.einsum(
        "rsn,snf->rf", scaled_piece, query_weights, preferred_element_type=jnp.float32
    )
    squares = jnp.sum(jnp.square(feature_piece.astype(jnp.float32)), axis=(1, 2))
    inverse_rms = lax.rsqrt(squares / D + NORM_EPS)
    queries = rotary(
        inverse_rms[:, None, None] * query_acc.reshape(local_rows, head_count, HD), query_within
    ).astype(jnp.bfloat16)
    scaled_local = (local_x.astype(jnp.float32) * gain_local[None]).astype(jnp.bfloat16)
    kv_partial = jnp.einsum(
        "rsw,swc->rc", scaled_local, w_keyval, preferred_element_type=jnp.float32
    )
    kv_total = lax.psum(kv_partial, "tp")
    head_block = lax.dynamic_slice_in_dim(kv_total, kv_head * 2 * HD, 2 * HD, 1)
    keys = rotary(inverse_rms[:, None, None] * head_block[:, None, :HD], query_within)[:, 0].astype(
        jnp.bfloat16
    )
    values = (inverse_rms[:, None] * head_block[:, HD:]).astype(jnp.bfloat16)
    score_scale = 1.0 / math.sqrt(HD)
    running = jnp.full((local_rows, head_count), MASK_FILL, jnp.float32)
    key_part = lax.all_gather(keys, "seq", axis=0, tiled=True)
    value_part = lax.all_gather(values, "seq", axis=0, tiled=True)
    key_count = key_part.shape[0]
    key_pos = jnp.arange(key_count, dtype=jnp.int32)
    key_seg = locate(key_pos, replica, tables)[0]
    allowed = (key_seg[None, :] == query_seg[:, None]) & query_valid[:, None] & (
        key_pos[None, :] <= query_pos[:, None]
    ) | (key_pos[None, :] == query_pos[:, None])
    scores = (
        jnp.einsum("rhd,kd->rhk", queries, key_part, preferred_element_type=jnp.float32)
        * score_scale
    )
    scores = jnp.where(allowed[:, None, :], scores, MASK_FILL)
    new_max = jnp.maximum(running, jnp.max(scores, axis=2))
    prob_terms = jnp.where(allowed[:, None, :], jnp.exp(scores - new_max[:, :, None]), 0.0)
    totals = jnp.sum(prob_terms, axis=2)
    accum = jnp.einsum(
        "rhk,kd->rhd",
        prob_terms.astype(jnp.bfloat16),
        value_part,
        preferred_element_type=jnp.float32,
    )
    attended = (
        (accum / totals[:, :, None]).reshape(local_rows, head_count * HD).astype(jnp.bfloat16)
    )
    return jnp.where(query_valid[:, None], attended, jnp.zeros((), jnp.bfloat16))


def solution(mesh):
    in_specs = (P("rep", ("seq", "tp")), P(), P("seq", "tp"), P(None, "tp", None), P(), P())
    out_specs = P(("rep", "seq"), "tp")
    return jax.shard_map(local, mesh=mesh, in_specs=in_specs, out_specs=out_specs, check_vma=False)
```

profile of v0, /device:TPU:16, one launch (start us, length us, event | category | flops | bytes accessed | tf_op | source)
XLA Modules:
  0.0 440.9 jit_solution(4229495986316716021)
XLA Ops:
  6.5 0.8 copy.25
  7.5 0.8 copy.24
  8.4 0.2 select_reduce_fusion.7
  9.1 3.5 gather_fusion
  12.7 1.3 select_select_fusion
  14.0 9.1 %all-to-all-start = ((bf16[8,192,128]{2,1,0:T(8,128)(2,1)}), bf16[8,192,128]{2,1,0:T(8,128)(2,1)S(1)}, u32[]{:S(2)}, u32[]{:S(2)}) async-start(bf16[8,192,128]{2,1,0:T(8,128)(2,1)} %select_select_fusion), calls=%async_computation | async-start | bytes 786432 | tf_op jit(solution)/shard_map/all_to_all | solution.py:107
  23.1 0.1 select_reduce_fusion.1
  23.3 9.1 %all-to-all-done = bf16[8,192,128]{2,1,0:T(8,128)(2,1)S(1)} async-done(((bf16[8,192,128]{2,1,0:T(8,128)(2,1)}), bf16[8,192,128]{2,1,0:T(8,128)(2,1)S(1)}, u32[]{:S(2)}, u32[]{:S(2)}) %all-to-all-start) | async-done | bytes 393248 | tf_op jit(solution)/shard_map/all_to_all | solution.py:107
  32.4 1.4 gather_fusion.1
  33.8 0.2 fusion.37
  34.0 0.5 broadcast.494
  34.5 0.7 reduce.4
  35.2 10.6 %all_to_all.27 = bf16[2,2,12288]{2,1,0:T(2,128)(2,1)S(1)} all-to-all(bf16[2,2,12288]{2,1,0:T(2,128)(2,1)S(1)} %reshape.481), channel_id=1, replica_groups=mesh['rep'=8,'seq'=2,'tp'=32] {'seq'}, dimensions={0} | all-to-all | bytes 196608 | tf_op jit(solution)/shard_map/all_to_all | solution.py:112
  45.9 0.7 copy.29
  46.6 0.7 all-gather.8.cloned.1.call-update
  47.6 0.2 fusion.18
  47.8 2.5 convolution_bitcast_fusion
  50.3 0.4 multiply_cosine_fusion.1
  50.7 82.6 %all-gather.6.cloned.1.call-done = bf16[192,2,1,4096]{3,0,1,2:T(8,128)(2,1)} async-done(((bf16[192,2,1,128]{3,0,1,2:T(8,128)(2,1)}), bf16[192,2,1,4096]{3,0,1,2:T(8,128)(2,1)}) %all-gather.6.cloned.1.call-update) | async-done | bytes 3145744 | tf_op jit(solution)/shard_map/all_gather | solution.py:126
  133.3 2.6 fusion
  135.9 111.5 %all-gather.8.cloned.1.call-done = bf16[8192,256]{1,0:T(8,128)(2,1)} async-done(((bf16[4096,256]{1,0:T(8,128)(2,1)}), bf16[8192,256]{1,0:T(8,128)(2,1)}) %all-gather.8.cloned.1.call-update) | async-done | bytes 4194320 | tf_op jit(solution)/shard_map/all_gather | solution.py:123
  247.4 4.1 fusion.7
  251.7 161.3 %all-reduce.2.cloned.1.call-done = f32[192,2048]{1,0:T(8,128)} async-done(((f32[192,2048]{1,0:T(8,128)}), f32[192,2048]{1,0:T(8,128)}) %all-reduce.2.cloned.1.call-update) | async-done | bytes 1572880 | tf_op jit(solution)/shard_map/psum | solution.py:140
  412.9 1.0 fusion.30
  413.9 0.5 fusion.26
  414.5 9.2 %all-gather.2 = bf16[384,1,128]{2,0,1:T(8,128)(2,1)S(1)} all-gather(bf16[192,1,128]{2,0,1:T(8,128)(2,1)S(1)} %pad_maximum_fusion), channel_id=4, replica_groups=mesh['rep'=8,'seq'=2,'tp'=32] {'seq'}, dimensions={0}, use_global_device_ids=true | all-gather | bytes 147456 | tf_op jit(solution)/shard_map/all_gather | solution.py:148
  423.7 0.1 subtract_convert_fusion
  423.9 0.4 fusion.50
  424.3 8.7 %all_gather.15 = bf16[384,128]{1,0:T(8,128)(2,1)S(1)} all-gather(bf16[192,128]{1,0:T(8,128)(2,1)S(1)} %get-tuple-element.19), channel_id=1, replica_groups=mesh['rep'=8,'seq'=2,'tp'=32] {'seq'}, dimensions={0}, use_global_device_ids=true | all-gather | bytes 147456 | tf_op jit(solution)/shard_map/all_gather | solution.py:149
  433.0 0.3 fusion.12
  433.3 0.3 fusion.11
  433.7 0.7 bitcast_select_fusion
  (41 shorter events, 1.4 us)
Async XLA Ops:
  6.5 41.2 %copy-start = (bf16[2,128,2048]{2,1,0:T(8,128)(2,1)S(1)}, bf16[2,128,2048]{2,1,0:T(8,128)(2,1)}, u32[]{:S(2)}) copy-start(bf16[2,128,2048]{2,1,0:T(8,128)(2,1)} %param.9) | copy-start | bytes 3145732
  12.7 34.7 %copy-start.1 = (f32[8192]{0:T(1024)S(1)}, f32[8192]{0:T(1024)}, u32[]{:S(2)}) copy-start(f32[8192]{0:T(1024)} %param.7) | copy-start | bytes 98308
  14.0 18.4 %all-to-all-start = ((bf16[8,192,128]{2,1,0:T(8,128)(2,1)}), bf16[8,192,128]{2,1,0:T(8,128)(2,1)S(1)}, u32[]{:S(2)}, u32[]{:S(2)}) async-start(bf16[8,192,128]{2,1,0:T(8,128)(2,1)} %select_select_fusion), calls=%async_computation | async-start | bytes 786432 | tf_op jit(solution)/shard_map/all_to_all | solution.py:107
  23.1 110.2 %all-gather.6.cloned.1.call-start = ((), (), s32[]{:S(2)}) async-start(), calls=%async_computation.3 | async-start | bytes 3244032 | tf_op jit(solution)/shard_map/all_gather | solution.py:126
  46.6 200.9 %all-gather.8.cloned.1.call-start = ((), (), s32[]{:S(2)}) async-start(), calls=%async_computation.4 | async-start | bytes 6291456 | tf_op jit(solution)/shard_map/all_gather | solution.py:123
  47.3 365.6 %all-reduce.2.cloned.1.call-start = ((), (), s32[]{:S(2)}) async-start(), calls=%async_computation.2 | async-start | bytes 3145728 | tf_op jit(solution)/shard_map/psum | solution.py:140
Sparse Core Ops, SparseCore 0:
  46.7 86.6 all-gather.5
  135.4 111.9 all-gather.7
  250.8 162.0 all-reduce.1
where the time goes:
time: 441 us
  waiting for transfers between devices  365 us (83%)
  blocking collectives  28.5 us (6%)
  between operations  13.4 us (3%)
  starting transfers between devices  9.17 us (2%)
  other arithmetic  9.02 us (2%)
  local copies, waits for them, and re-layouts  8.3 us (2%)
  matrix products  7.34 us (2%)
    psum x1, waiting for transfers between devices, local(): kv_total = lax.psum(kv_partial, 'tp')  161 us
    all_gather x1, waiting for transfers between devices, local(): lax.all_gather(w_query.reshape(1, w_query.shape[0], w_query.shape[1]), 's...  111 us
    all_gather x1, waiting for transfers between devices, local(): feature_piece = lax.all_gather(local_x, 'tp', axis=2, tiled=True)  82.6 us
    all_to_all x1, blocking collectives, local(): lax.all_to_all(assembled.reshape(BUFFER, 1, feature_cols), 'seq', split_a...  10.6 us
    all_gather x1, blocking collectives, local(): key_part = lax.all_gather(keys, 'seq', axis=0, tiled=True)  9.25 us
    all_to_all x1, waiting for transfers between devices, local(): lax.all_to_all(outgoing, 'rep', split_axis=0, concat_axis=0, tiled=True)  9.09 us
    all_to_all x1, starting transfers between devices, local(): lax.all_to_all(outgoing, 'rep', split_axis=0, concat_axis=0, tiled=True)  9.08 us
  transfers between devices with their start and end apart: 4, of which 4 were waited for; matrix products, arithmetic and copies ran while one was open for 2% of the time, Pallas kernels for 0%

commit v1 on v0

--- a/solution.py
+++ b/solution.py
@@ -14,6 +14,10 @@
 ROPE_BASE = 500000.0
 NORM_EPS = 1e-05
 MASK_FILL = -1e30
+
+
+def strings_recover(payload):
+    return lax.all_gather(payload, axis_name="tp").sum(axis=0)
 
 
 def response_tables(lengths, routes):
@@ -137,7 +141,7 @@
     kv_partial = jnp.einsum(
         "rsw,swc->rc", scaled_local, w_keyval, preferred_element_type=jnp.float32
     )
-    kv_total = lax.psum(kv_partial, "tp")
+    kv_total = strings_recover(kv_partial)
     head_block = lax.dynamic_slice_in_dim(kv_total, kv_head * 2 * HD, 2 * HD, 1)
     keys = rotary(inverse_rms[:, None, None] * head_block[:, None, :HD], query_within)[:, 0].astype(
         jnp.bfloat16

time: 441 us -> 633 us (1.44)
  waiting for transfers between devices: 365 us -> 540 us
  other arithmetic: 9.02 us -> 25.2 us
    all_gather x0 -> x1, waiting for transfers between devices: none -> 337 us  [strings_recover(): return lax.all_gather(payload, axis_name='tp').sum(axis=0)]
    psum x1 -> x0, waiting for transfers between devices: 161 us -> none  [local(): kv_total = lax.psum(kv_partial, 'tp')]
    reduce_sum x0 -> x1, other arithmetic: none -> 17.1 us  [strings_recover(): return lax.all_gather(payload, axis_name='tp').sum(axis=0)]
where the time goes in v1:
time: 633 us; the launch traced here: 632 us
  waiting for transfers between devices  540 us (85%)
  blocking collectives  28.5 us (5%)
  other arithmetic  25.2 us (4%)
  between operations  13.4 us (2%)
  starting transfers between devices  9.17 us (1%)
  local copies, waits for them, and re-layouts  8.31 us (1%)
  matrix products  7.37 us (1%)
    all_gather x1, waiting for transfers between devices, strings_recover(): return lax.all_gather(payload, axis_name='tp').sum(axis=0)  337 us
    all_gather x1, waiting for transfers between devices, local(): lax.all_gather(w_query.reshape(1, w_query.shape[0], w_query.shape[1]), 's...  111 us
    all_gather x1, waiting for transfers between devices, local(): feature_piece = lax.all_gather(local_x, 'tp', axis=2, tiled=True)  82.6 us
    reduce_sum x1, other arithmetic, strings_recover(): return lax.all_gather(payload, axis_name='tp').sum(axis=0)  17.1 us
  transfers between devices with their start and end apart: 4, of which 4 were waited for; matrix products, arithmetic and copies ran while one was open for 2% of the time, Pallas kernels for 0%

profile of v1, /device:TPU:16, one launch (start us, length us, event | category | flops | bytes accessed | tf_op | source)
XLA Modules:
  0.0 632.4 jit_solution(15979443122288139436)
XLA Ops:
  6.5 0.8 copy.25
  7.5 0.8 copy.24
  8.4 0.2 select_reduce_fusion.7
  9.1 3.5 gather_fusion
  12.7 1.3 select_select_fusion
  14.0 9.1 %all-to-all-start = ((bf16[8,192,128]{2,1,0:T(8,128)(2,1)}), bf16[8,192,128]{2,1,0:T(8,128)(2,1)S(1)}, u32[]{:S(2)}, u32[]{:S(2)}) async-start(bf16[8,192,128]{2,1,0:T(8,128)(2,1)} %select_select_fusion), calls=%async_computation | async-start | bytes 786432 | tf_op jit(solution)/shard_map/all_to_all | solution.py:111
  23.1 0.1 select_reduce_fusion.1
  23.3 9.1 %all-to-all-done = bf16[8,192,128]{2,1,0:T(8,128)(2,1)S(1)} async-done(((bf16[8,192,128]{2,1,0:T(8,128)(2,1)}), bf16[8,192,128]{2,1,0:T(8,128)(2,1)S(1)}, u32[]{:S(2)}, u32[]{:S(2)}) %all-to-all-start) | async-done | bytes 393248 | tf_op jit(solution)/shard_map/all_to_all | solution.py:111
  32.4 1.4 gather_fusion.1
  33.8 0.2 fusion.37
  34.0 0.5 broadcast.494
  34.5 0.7 reduce.4
  35.2 10.6 %all_to_all.27 = bf16[2,2,12288]{2,1,0:T(2,128)(2,1)S(1)} all-to-all(bf16[2,2,12288]{2,1,0:T(2,128)(2,1)S(1)} %reshape.482), channel_id=1, replica_groups=mesh['rep'=8,'seq'=2,'tp'=32] {'seq'}, dimensions={0} | all-to-all | bytes 196608 | tf_op jit(solution)/shard_map/all_to_all | solution.py:116
  45.9 0.7 copy.29
  46.6 0.7 all-gather.10.cloned.1.call-update
  47.4 2.5 convolution_bitcast_fusion
  50.1 0.2 fusion.18
  50.3 0.4 multiply_cosine_fusion.1
  50.7 82.6 %all-gather.8.cloned.1.call-done = bf16[192,2,1,4096]{3,0,1,2:T(8,128)(2,1)} async-done(((bf16[192,2,1,128]{3,0,1,2:T(8,128)(2,1)}), bf16[192,2,1,4096]{3,0,1,2:T(8,128)(2,1)}) %all-gather.8.cloned.1.call-update) | async-done | bytes 3145744 | tf_op jit(solution)/shard_map/all_gather | solution.py:130
  133.3 2.6 fusion
  135.9 111.5 %all-gather.10.cloned.1.call-done = bf16[8192,256]{1,0:T(8,128)(2,1)} async-done(((bf16[4096,256]{1,0:T(8,128)(2,1)}), bf16[8192,256]{1,0:T(8,128)(2,1)}) %all-gather.10.cloned.1.call-update) | async-done | bytes 4194320 | tf_op jit(solution)/shard_map/all_gather | solution.py:127
  247.4 4.1 fusion.7
  251.7 0.1 subtract_convert_fusion
  251.8 336.6 %all-gather.12.cloned.1.call-done = f32[6144,2048]{1,0:T(8,128)} async-done(((f32[192,2048]{1,0:T(8,128)}), f32[6144,2048]{1,0:T(8,128)}) %all-gather.12.cloned.1.call-update) | async-done | bytes 50331664 | tf_op jit(solution)/shard_map/all_gather | solution.py:20
  588.4 17.1 %reduce_sum.125 = f32[192,2048]{1,0:T(8,128)S(1)} reduce(f32[32,192,2048]{2,1,0:T(8,128)} %bitcast.48, f32[]{:T(128)} %constant.113.clone.1), dimensions={0}, to_apply=%region_11.12 | reduce | flops 12189696 | bytes 51904516 | tf_op jit(solution)/shard_map/reduce_sum | solution.py:20
  605.6 0.5 fusion.26
  606.1 9.2 %all-gather.3 = bf16[384,1,128]{2,0,1:T(8,128)(2,1)S(1)} all-gather(bf16[192,1,128]{2,0,1:T(8,128)(2,1)S(1)} %pad_maximum_fusion), channel_id=5, replica_groups=mesh['rep'=8,'seq'=2,'tp'=32] {'seq'}, dimensions={0}, use_global_device_ids=true | all-gather | bytes 147456 | tf_op jit(solution)/shard_map/all_gather | solution.py:152
  615.4 0.4 fusion.50
  615.8 8.7 %all_gather.23 = bf16[384,128]{1,0:T(8,128)(2,1)S(1)} all-gather(bf16[192,128]{1,0:T(8,128)(2,1)S(1)} %get-tuple-element.19), channel_id=1, replica_groups=mesh['rep'=8,'seq'=2,'tp'=32] {'seq'}, dimensions={0}, use_global_device_ids=true | all-gather | bytes 147456 | tf_op jit(solution)/shard_map/all_gather | solution.py:153
  624.5 0.3 fusion.12
  624.8 0.3 fusion.11
  625.1 0.7 bitcast_select_fusion
  (44 shorter events, 1.5 us)
Async XLA Ops:
  6.5 40.9 %copy-start = (bf16[2,128,2048]{2,1,0:T(8,128)(2,1)S(1)}, bf16[2,128,2048]{2,1,0:T(8,128)(2,1)}, u32[]{:S(2)}) copy-start(bf16[2,128,2048]{2,1,0:T(8,128)(2,1)} %param.9) | copy-start | bytes 3145732
  12.7 34.7 %copy-start.2 = (f32[8192]{0:T(1024)S(1)}, f32[8192]{0:T(1024)}, u32[]{:S(2)}) copy-start(f32[8192]{0:T(1024)} %param.7) | copy-start | bytes 98308
  14.0 18.4 %all-to-all-start = ((bf16[8,192,128]{2,1,0:T(8,128)(2,1)}), bf16[8,192,128]{2,1,0:T(8,128)(2,1)S(1)}, u32[]{:S(2)}, u32[]{:S(2)}) async-start(bf16[8,192,128]{2,1,0:T(8,128)(2,1)} %select_select_fusion), calls=%async_computation | async-start | bytes 786432 | tf_op jit(solution)/shard_map/all_to_all | solution.py:111
  23.1 110.2 %all-gather.8.cloned.1.call-start = ((), (), s32[]{:S(2)}) async-start(), calls=%async_computation.2 | async-start | bytes 3244032 | tf_op jit(solution)/shard_map/all_gather | solution.py:130
  46.6 200.9 %all-gather.10.cloned.1.call-start = ((), (), s32[]{:S(2)}) async-start(), calls=%async_computation.3 | async-start | bytes 6291456 | tf_op jit(solution)/shard_map/all_gather | solution.py:127
  47.3 541.1 %all-gather.12.cloned.1.call-start = ((), (), s32[]{:S(2)}) async-start(), calls=%async_computation.4 | async-start | bytes 51904512 | tf_op jit(solution)/shard_map/all_gather | solution.py:20
  588.4 37.5 %copy-start.1 = (bf16[2,128,2048]{2,1,0:T(8,128)(2,1)S(1)}, bf16[2,128,2048]{2,1,0:T(8,128)(2,1)}, u32[]{:S(2)}) copy-start(bf16[2,128,2048]{2,1,0:T(8,128)(2,1)} %param.9) | copy-start | bytes 3145732
Sparse Core Ops, SparseCore 0:
  46.7 86.6 all-gather.7
  135.4 111.9 all-gather.9
  250.6 337.7 all-gather.11
